TPU v7x, 512 devices: a whole 4x4x16 slice. The times are simulated.
512 devices in a mesh: ctx: 64 (over z_lo, y, core), wa: 8 (over z_hi, x).
Axes of the slice: x: 4, y: 4, z: 16 (z_hi: 2, z_lo: 8; z = z_hi * 8 + z_lo), core: 2. Of those that a mesh axis runs over, the one named last changes fastest.
Arguments:
- q_nope: bfloat16 [512, 8192], P('ctx', 'wa'), may hold values from -6 to 6
- q_rope: bfloat16 [512, 4096], P('ctx', 'wa'), may hold values from -100 to 100
- w_uk: bfloat16 [64, 128, 512], P('wa'), may hold values from -0.25 to 0.25
- w_uv: bfloat16 [64, 512, 128], P('wa'), may hold values from -0.25 to 0.25
- cache: bfloat16 [32768, 576], P('ctx'), may hold values from -16 to 16
- cache_scale: float32 [32768], P('ctx'), may hold values from 0.5 to 2, as said below
- new_latent: bfloat16 [512, 576], P('ctx'), may hold values from -16 to 16
- cache_doc: int32 [512], P('ctx'), may hold values from 0 to 15
- new_lengths: int32 [16], replicated, may hold values from 1 to 128, 512 in all
Outputs:
- attn_out: bfloat16 [512, 8192], P('ctx', 'wa')
Inputs may be any that keep to these rules, and one draw needn't show every extreme that they name: `cache_scale`: each scale is 0.5, 1 or 2.
All inputs are finite; a program needn't handle non-finite values.
Results may differ from a plain program's by a relative error of at most 0.0064.
Values may be sent and summed in bfloat16 or wider, within the bound.
No kernel may reach another device: no remote copies, remote signals or barrier semaphores. Data moves between devices by JAX's collectives and lax.ppermute only.
A program may use at most 64 MiB of HBM per device.

v0:
```python
import jax
import jax.numpy as jnp
from jax import lax
from jax.sharding import PartitionSpec as P


def doc_index(position, new_lengths):
    ends = jnp.cumsum(new_lengths)
    return jnp.sum((ends[None, :] <= position[:, None]).astype(jnp.int32), axis=1)


def absorb_rows(nope_rows, w_uk):
    row_count = nope_rows.shape[0]
    heads_dev, nope_dim, latent_dim = w_uk.shape
    shaped = nope_rows.reshape(row_count, heads_dev, nope_dim)
    absorbed = jnp.einsum("thn,hnl->thl", shaped, w_uk, preferred_element_type=jnp.float32)
    return absorbed.astype(jnp.bfloat16)


def body(q_nope, q_rope, w_uk, w_uv, cache, cache_scale, new_latent, cache_doc, new_lengths):
    tok_rows = q_nope.shape[0]
    heads_dev, nope_dim, latent_dim = w_uk.shape
    value_dim = w_uv.shape[2]
    rope_dim = q_rope.shape[1] // heads_dev
    shards = lax.axis_size("ctx")
    all_rows = tok_rows * shards
    my_index = lax.axis_index("ctx")
    score_scale = (nope_dim + rope_dim) ** (-0.5)
    own_q = jnp.concatenate([q_nope, q_rope], axis=1)
    all_q = lax.all_gather(own_q, "ctx", axis=0, tiled=True)
    nope_width = heads_dev * nope_dim
    all_lat = absorb_rows(all_q[:, :nope_width], w_uk)
    all_rope = all_q[:, nope_width:]
    query = jnp.concatenate([all_lat, all_rope.reshape(all_rows, heads_dev, rope_dim)], axis=2)
    dequant = (cache.astype(jnp.float32) * cache_scale[:, None]).astype(jnp.bfloat16)
    key_rows = jnp.concatenate([dequant, new_latent], axis=0)
    cache_len = cache.shape[0]
    block_len = cache_len // cache_doc.shape[0]
    query_pos = jnp.arange(all_rows, dtype=jnp.int32)
    query_doc = doc_index(query_pos, new_lengths)
    new_pos = my_index * tok_rows + jnp.arange(tok_rows, dtype=jnp.int32)
    key_doc = jnp.concatenate([jnp.repeat(cache_doc, block_len), doc_index(new_pos, new_lengths)])
    key_pos = jnp.concatenate([jnp.full((cache_len,), -1, dtype=jnp.int32), new_pos])
    allowed = (query_doc[:, None] == key_doc[None, :]) & (key_pos[None, :] <= query_pos[:, None])
    score = (
        jnp.einsum("qhl,kl->qhk", query, key_rows, preferred_element_type=jnp.float32) * score_scale
    )
    masked = jnp.where(allowed[:, None, :], score, -jnp.inf)
    local_max = jnp.max(masked, axis=2)
    shift = jnp.where(jnp.isfinite(local_max), local_max, jnp.zeros_like(local_max))
    weight = jnp.exp(masked - shift[:, :, None])
    totals = jnp.sum(weight, axis=2)
    weight_low = weight.astype(jnp.bfloat16)
    part_lat = jnp.einsum(
        "qhk,kl->qhl", weight_low, key_rows[:, :latent_dim], preferred_element_type=jnp.float32
    ).astype(jnp.bfloat16)
    numerator = jnp.einsum("qhl,hlv->qhv", part_lat, w_uv, preferred_element_type=jnp.float32)
    stats = lax.all_gather(jnp.concatenate([local_max, totals], axis=1), "ctx", axis=0, tiled=False)
    row_max = jnp.max(stats[:, :, :heads_dev], axis=0)
    factor = jnp.exp(local_max - row_max)
    scaled = (numerator * factor[:, :, None]).reshape(all_rows, heads_dev * value_dim)
    own_numer = lax.psum_scatter(scaled, "ctx", scatter_dimension=0, tiled=True)
    own_numer = own_numer.reshape(tok_rows, heads_dev, value_dim)
    own_stats = lax.dynamic_slice_in_dim(stats, my_index * tok_rows, tok_rows, axis=1)
    own_max = lax.dynamic_slice_in_dim(row_max, my_index * tok_rows, tok_rows, axis=0)
    own_factor = jnp.exp(own_stats[:, :, :heads_dev] - own_max[None])
    own_total = jnp.sum(own_factor * own_stats[:, :, heads_dev:], axis=0)
    result = own_numer / own_total[:, :, None]
    return result.astype(jnp.bfloat16).reshape(tok_rows, heads_dev * value_dim)


def solution(mesh):
    placed = (
        P("ctx", "wa"),
        P("ctx", "wa"),
        P("wa", None, None),
        P("wa", None, None),
        P("ctx", None),
        P("ctx"),
        P("ctx", None),
        P("ctx"),
        P(),
    )
    return jax.shard_map(
        body, mesh=mesh, in_specs=placed, out_specs=P("ctx", "wa"), check_vma=False
    )
```

profile of v0, /device:TPU:2, one launch (start us, length us, event | category | flops | bytes accessed | tf_op | source)
XLA Modules:
  0.0 727.8 jit_solution(12860980277982599046)
XLA Ops:
  6.5 1.4 pad_maximum_fusion.2
  8.0 0.0 all-gather.6.cloned.1.call-start
  8.0 0.7 copy.42
  8.8 0.1 reduce
  8.9 0.7 broadcast_in_dim.12
  9.7 0.1 reshape.99
  9.7 1.5 copy.47
  11.2 0.2 convert_reduce_fusion.1
  11.4 0.1 convert_reduce_fusion
  11.5 0.3 fusion.23
  11.8 2.0 multiply_convert_fusion
  13.8 120.8 %all-gather.4.cloned.1.call-done = bf16[512,1536]{1,0:T(8,128)(2,1)} async-done(((bf16[8,1536]{1,0:T(8,128)(2,1)}), bf16[512,1536]{1,0:T(8,128)(2,1)}) %all-gather.4.cloned.1.call-update) | async-done | bytes 1572880 | tf_op jit(solution)/shard_map/all_gather | solution.py:30
  134.6 1.3 slice.24
  135.9 0.5 copy.59
  136.5 1.1 slice.25
  137.6 1.0 copy.46
  138.6 1.3 convert_bitcast_fusion
  140.0 4.7 fusion
  144.7 1.7 fusion.1
  146.4 1.5 copy-done.1
  147.9 0.6 pad_maximum_fusion.1
  148.5 0.0 all-gather.6.cloned.1.call-update
  148.6 0.2 reduce-scatter.2.cloned.1.call-start
  148.8 116.5 %all-gather.6.cloned.1.call-done = f32[32768,16]{0,1:T(8,128)} async-done(((f32[512,16]{0,1:T(8,128)}), f32[32768,16]{0,1:T(8,128)}) %all-gather.6.cloned.1.call-update) | async-done | bytes 2097168 | tf_op jit(solution)/shard_map/all_gather | solution.py:58
  265.3 2.8 copy.60
  268.1 0.1 slice_reduce_fusion
  268.2 10.4 %bitcast_multiply_fusion = f32[512,8,128]{0,2,1:T(8,128)} fusion(bf16[8,512,128]{2,1,0:T(8,128)(2,1)} %param.12, f32[512,8,520]{0,2,1:T(8,128)} %copy-done.1, f32[512,8]{0,1:T(8,128)S(1)} %is-finite_select_fusion, pred[512,520]{0,1:T(8,128)(4,1)S(1)} %fusion.23, f32[512,8]{0,1:T(8,128)S(1)} %subtract_exponential_fusion.1, ...), kind=kOutput, calls=%fused_computation.17 | convolution fusion | flops 2730115072 | bytes 12563456 | tf_op jit(solution)/shard_map/qhl,hlv->qhv/dot_general | solution.py:57
  278.6 2.9 copy.51
  281.5 0.1 constant_dynamic-slice_fusion
  281.6 0.2 fusion.31
  281.8 438.0 %reduce-scatter.2.cloned.1.call-done = f32[8,1024]{1,0:T(8,128)} async-done(((f32[512,1024]{1,0:T(8,128)}), f32[8,1024]{1,0:T(8,128)}) %reduce-scatter.2.cloned.1.call-update) | async-done | bytes 32784 | tf_op jit(solution)/shard_map/reduce_scatter | solution.py:62
  719.8 1.4 fusion.33
  (18 shorter events, 0.1 us)
Async XLA Ops:
  6.5 132.1 %copy-start = (bf16[8,128,512]{2,1,0:T(8,128)(2,1)S(1)}, bf16[8,128,512]{2,1,0:T(8,128)(2,1)}, u32[]{:S(2)}) copy-start(bf16[8,128,512]{2,1,0:T(8,128)(2,1)} %param.11) | copy-start | bytes 3145732
  6.5 128.1 %all-gather.4.cloned.1.call-start = ((), (), s32[]{:S(2)}) async-start(), calls=%async_computation.1 | async-start | bytes 1597440 | tf_op jit(solution)/shard_map/all_gather | solution.py:30
  8.0 257.3 %all-gather.6.cloned.1.call-start = ((), (), s32[]{:S(2)}) async-start(), calls=%async_computation.3 | async-start | bytes 2129920 | tf_op jit(solution)/shard_map/all_gather | solution.py:58
  136.5 3.4 copy-start.4
  138.6 1.3 copy-start.2
  138.6 1.3 copy-start.3
  144.6 3.3 copy-start.1
  148.6 571.3 %reduce-scatter.2.cloned.1.call-start = ((), (), s32[]{:S(2)}) async-start(), calls=%async_computation.2 | async-start | bytes 2129920 | tf_op jit(solution)/shard_map/reduce_scatter | solution.py:62
Sparse Core Ops, SparseCore 0:
  9.5 125.1 all-gather.3
  148.7 116.5 all-gather.5
  281.7 438.1 reduce-scatter.1
where the time goes:
time: 728 us
  waiting for transfers between devices  675 us (93%)
  matrix products  16.3 us (2%)
  local copies, waits for them, and re-layouts  14.3 us (2%)
  between operations  13.2 us (2%)
  other arithmetic  8.3 us (1%)
    reduce_scatter x1, waiting for transfers between devices, body(): own_numer = lax.psum_scatter(scaled, 'ctx', scatter_dimension=0, tiled=True)  438 us
    all_gather x1, waiting for transfers between devices, body(): all_q = lax.all_gather(own_q, 'ctx', axis=0, tiled=True)  121 us
    all_gather x1, waiting for transfers between devices, body(): lax.all_gather(jnp.concatenate([local_max, totals], axis=1), 'ctx', axis=...  116 us
  transfers between devices with their start and end apart: 3, of which 3 were waited for; matrix products, arithmetic and copies ran while one was open for 1% of the time, Pallas kernels for 0%

commit v1 on v0

--- a/solution.py
+++ b/solution.py
@@ -27,7 +27,9 @@
     my_index = lax.axis_index("ctx")
     score_scale = (nope_dim + rope_dim) ** (-0.5)
     own_q = jnp.concatenate([q_nope, q_rope], axis=1)
-    all_q = lax.all_gather(own_q, "ctx", axis=0, tiled=True)
+    part_now = jnp.stack([own_q] * lax.axis_size("ctx"))
+    formed = lax.all_to_all(part_now, "ctx", 0, 0)
+    all_q = jnp.concatenate(formed, axis=0)
     nope_width = heads_dev * nope_dim
     all_lat = absorb_rows(all_q[:, :nope_width], w_uk)
     all_rope = all_q[:, nope_width:]

time: 728 us -> 694 us (0.953)
  waiting for transfers between devices: 675 us -> 626 us
  starting transfers between devices: 0.27 us -> 16.4 us
    all_gather x1 -> x0, waiting for transfers between devices: 121 us -> none  [body(): all_q = lax.all_gather(own_q, 'ctx', axis=0, tiled=True)]
    all_to_all x0 -> x1, waiting for transfers between devices: none -> 70 us  [body(): formed = lax.all_to_all(part_now, 'ctx', 0, 0)]
    all_to_all x0 -> x1, starting transfers between devices: none -> 16.2 us  [body(): formed = lax.all_to_all(part_now, 'ctx', 0, 0)]
where the time goes in v1:
time: 694 us; the launch traced here: 693 us
  waiting for transfers between devices  626 us (90%)
  matrix products  17.4 us (3%)
  starting transfers between devices  16.4 us (2%)
  between operations  13.6 us (2%)
  local copies, waits for them, and re-layouts  12.5 us (2%)
  other arithmetic  7.7 us (1%)
    reduce_scatter x1, waiting for transfers between devices, body(): own_numer = lax.psum_scatter(scaled, 'ctx', scatter_dimension=0, tiled=True)  438 us
    all_gather x1, waiting for transfers between devices, body(): lax.all_gather(jnp.concatenate([local_max, totals], axis=1), 'ctx', axis=...  118 us
    all_to_all x1, waiting for transfers between devices, body(): formed = lax.all_to_all(part_now, 'ctx', 0, 0)  70 us
    all_to_all x1, starting transfers between devices, body(): formed = lax.all_to_all(part_now, 'ctx', 0, 0)  16.2 us
  transfers between devices with their start and end apart: 3, of which 3 were waited for; matrix products, arithmetic and copies ran while one was open for 1% of the time, Pallas kernels for 0%

profile of v1, /device:TPU:2, one launch (start us, length us, event | category | flops | bytes accessed | tf_op | source)
XLA Modules:
  0.0 693.2 jit_solution(643382706939654967)
XLA Ops:
  6.5 0.8 pad_maximum_fusion.2
  7.4 1.3 stack.2
  8.6 16.2 %all-to-all-start = ((bf16[64,8,1536]{2,1,0:T(8,128)(2,1)}), bf16[64,8,1536]{2,1,0:T(8,128)(2,1)S(1)}, u32[]{:S(2)}, u32[]{:S(2)}) async-start(bf16[64,8,1536]{2,1,0:T(8,128)(2,1)} %stack.2), calls=%async_computation | async-start | bytes 3145728 | tf_op jit(solution)/shard_map/all_to_all | solution.py:31
  24.8 0.0 all-gather.3.cloned.1.call-start
  24.9 0.1 copy.34
  25.0 0.1 reduce
  25.1 0.1 broadcast_in_dim.12
  25.2 0.1 reshape.104
  25.3 0.8 copy.39
  26.1 0.2 convert_reduce_fusion.1
  26.3 0.1 convert_reduce_fusion
  26.3 0.3 fusion.23
  26.7 2.0 multiply_convert_fusion
  28.7 70.0 %all-to-all-done = bf16[64,8,1536]{2,1,0:T(8,128)(2,1)S(1)} async-done(((bf16[64,8,1536]{2,1,0:T(8,128)(2,1)}), bf16[64,8,1536]{2,1,0:T(8,128)(2,1)S(1)}, u32[]{:S(2)}, u32[]{:S(2)}) %all-to-all-start) | async-done | bytes 1572896 | tf_op jit(solution)/shard_map/all_to_all | solution.py:31
  98.6 1.1 slice.24
  99.8 1.5 copy.35
  101.3 0.2 copy.38
  101.5 1.3 convert_bitcast_fusion
  102.8 5.7 fusion
  108.6 1.7 fusion.1
  110.3 1.5 copy-done.1
  111.8 0.6 pad_maximum_fusion.1
  112.5 0.2 reduce-scatter.2.cloned.1.call-start
  112.7 117.7 %all-gather.3.cloned.1.call-done = f32[32768,16]{0,1:T(8,128)} async-done(((f32[512,16]{0,1:T(8,128)}), f32[32768,16]{0,1:T(8,128)}) %all-gather.3.cloned.1.call-update) | async-done | bytes 2097168 | tf_op jit(solution)/shard_map/all_gather | solution.py:60
  230.4 2.8 copy.51
  233.2 0.1 slice_reduce_fusion
  233.3 10.4 %bitcast_multiply_fusion = f32[512,8,128]{0,2,1:T(8,128)} fusion(bf16[8,512,128]{2,1,0:T(8,128)(2,1)} %param.12, f32[512,8,520]{0,2,1:T(8,128)} %copy-done.1, f32[512,8]{0,1:T(8,128)S(1)} %is-finite_select_fusion, pred[512,520]{0,1:T(8,128)(4,1)S(1)} %fusion.23, f32[512,8]{0,1:T(8,128)S(1)} %subtract_exponential_fusion.1, ...), kind=kOutput, calls=%fused_computation.17 | convolution fusion | flops 2730115072 | bytes 12563456 | tf_op jit(solution)/shard_map/qhl,hlv->qhv/dot_general | solution.py:59
  243.7 2.9 copy.43
  246.7 0.1 constant_dynamic-slice_fusion
  246.7 0.2 fusion.31
  247.0 437.9 %reduce-scatter.2.cloned.1.call-done = f32[8,1024]{1,0:T(8,128)} async-done(((f32[512,1024]{1,0:T(8,128)}), f32[8,1024]{1,0:T(8,128)}) %reduce-scatter.2.cloned.1.call-update) | async-done | bytes 32784 | tf_op jit(solution)/shard_map/reduce_scatter | solution.py:64
  684.9 1.4 fusion.33
  (22 shorter events, 0.2 us)
Async XLA Ops:
  6.5 95.0 %copy-start = (bf16[8,128,512]{2,1,0:T(8,128)(2,1)S(1)}, bf16[8,128,512]{2,1,0:T(8,128)(2,1)}, u32[]{:S(2)}) copy-start(bf16[8,128,512]{2,1,0:T(8,128)(2,1)} %param.11) | copy-start | bytes 3145732
  6.5 18.3 %copy-start.5 = (s32[16]{0:T(128)S(1)}, s32[16]{0:T(128)}, u32[]{:S(2)}) copy-start(s32[16]{0:T(128)} %param.17) | copy-start | bytes 196
  6.5 18.6 %copy-start.6 = (s32[8]{0:T(128)S(1)}, s32[8]{0:T(128)}, u32[]{:S(2)}) copy-start(s32[8]{0:T(128)} %param.16) | copy-start | bytes 100
  6.5 18.7 %copy-start.3 = (bf16[8,576]{1,0:T(8,128)(2,1)S(1)}, bf16[8,576]{1,0:T(8,128)(2,1)}, u32[]{:S(2)}) copy-start(bf16[8,576]{1,0:T(8,128)(2,1)} %param.15) | copy-start | bytes 27652
  6.5 20.1 %copy-start.4 = (f32[512]{0:T(512)S(1)}, f32[512]{0:T(512)}, u32[]{:S(2)}) copy-start(f32[512]{0:T(512)} %param.14) | copy-start | bytes 6148
  8.6 90.0 %all-to-all-start = ((bf16[64,8,1536]{2,1,0:T(8,128)(2,1)}), bf16[64,8,1536]{2,1,0:T(8,128)(2,1)S(1)}, u32[]{:S(2)}, u32[]{:S(2)}) async-start(bf16[64,8,1536]{2,1,0:T(8,128)(2,1)} %stack.2), calls=%async_computation | async-start | bytes 3145728 | tf_op jit(solution)/shard_map/all_to_all | solution.py:31
  24.8 205.6 %all-gather.3.cloned.1.call-start = ((), (), s32[]{:S(2)}) async-start(), calls=%async_computation.3 | async-start | bytes 2129920 | tf_op jit(solution)/shard_map/all_gather | solution.py:60
  101.5 1.3 copy-start.2
  108.6 3.3 copy-start.1
  112.5 572.4 %reduce-scatter.2.cloned.1.call-start = ((), (), s32[]{:S(2)}) async-start(), calls=%async_computation.2 | async-start | bytes 2129920 | tf_op jit(solution)/shard_map/reduce_scatter | solution.py:64
Sparse Core Ops, SparseCore 0:
  112.6 117.7 all-gather.2
  246.8 438.0 reduce-scatter.1
